TPU v7x, 256 devices: a whole 4x4x8 slice. The times are simulated.
256 devices in a mesh: section: 2 (over x_hi), ctx: 32 (over z, x_lo, core), mp: 4 (over y).
Axes of the slice: x: 4 (x_hi: 2, x_lo: 2; x = x_hi * 2 + x_lo), y: 4, z: 8, core: 2. Of those that a mesh axis runs over, the one named last changes fastest.
Arguments:
- queries: bfloat16 [2, 8192, 4096], P('section', 'ctx', 'mp'), may hold values from -130 to 130
- keys: bfloat16 [2, 8192, 512], P('section', 'ctx', 'mp'), may hold values from -4.5 to 4.5
- values: bfloat16 [2, 8192, 512], P('section', 'ctx', 'mp'), may hold values from -6 to 6
- doc_lengths: int32 [2, 16], P('section'), may hold values from 1 to 4096, 8192 in all within a row
Outputs:
- attended: bfloat16 [2, 8192, 4096], P('section', ('ctx', 'mp'))
- passed: bfloat16 [2, 8192, 4096], P('section', ('ctx', 'mp'))
All inputs are finite; a program needn't handle non-finite values.
Results may differ from a plain program's by a relative error of at most 0.004.
Values may be sent and summed in bfloat16 or wider, within the bound.
No kernel may reach another device: no remote copies, remote signals or barrier semaphores. Data moves between devices by JAX's collectives and lax.ppermute only.
A program may use at most 192 MiB of HBM per device.

v0:
```python
import math
import jax
import jax.numpy as jnp
from jax import lax
from jax.sharding import PartitionSpec as P

DH = 128
DOCS = 16


def from_behind(block, axis, distance):
    devices = range(lax.axis_size(axis))
    route = [((i - distance) % len(devices), i) for i in devices]
    return lax.ppermute(block, axis, route)


def doc_of(positions, ends):
    return jnp.sum((positions[:, None] >= ends[None, :]).astype(jnp.int32), axis=1)


def body(queries, keys, values, doc_lengths):
    query_rows = queries[0]
    key_rows = keys[0]
    value_rows = values[0]
    lengths = doc_lengths[0]
    rows = query_rows.shape[0]
    kv_heads = key_rows.shape[1] // DH
    heads = query_rows.shape[1] // DH
    group = heads // kv_heads
    cycle = lax.axis_size("ctx")
    base_len = rows * cycle // 16
    position = lax.axis_index("ctx")
    first = position * rows
    ends = jnp.cumsum(lengths)
    query_pos = first + jnp.arange(rows, dtype=jnp.int32)
    query_doc = doc_of(query_pos, ends)
    lookup = query_doc[:, None] == jnp.arange(DOCS, dtype=jnp.int32)[None, :]
    query_len = jnp.sum(jnp.where(lookup, lengths[None, :], 0), axis=1).astype(jnp.float32)
    factor = jnp.maximum(1.0, jnp.log(query_len) / math.log(float(base_len))) * (
        1.0 / math.sqrt(DH)
    )
    query_heads = query_rows.reshape(rows, kv_heads, group, DH)
    key_piece = lax.all_gather(key_rows, "ctx", axis=0, tiled=True)
    value_piece = lax.all_gather(value_rows, "ctx", axis=0, tiled=True)
    top = jnp.full((kv_heads, group, rows), -1e30, jnp.float32)
    count = key_piece.shape[0]
    key_pos = jnp.arange(count, dtype=jnp.int32)
    key_doc = doc_of(key_pos, ends)
    score = jnp.einsum(
        "qhgd,khd->hgqk",
        query_heads,
        key_piece.reshape(count, kv_heads, DH),
        preferred_element_type=jnp.float32,
    )
    score = score * factor[None, None, :, None]
    allowed = (
        (query_doc[:, None] == key_doc[None, :])
        & (key_pos[None, :] <= query_pos[:, None])
        & (key_pos[None, :] >= 0)
    )
    score = jnp.where(allowed[None, None], score, -1e30)
    new_top = jnp.maximum(top, jnp.max(score, axis=-1))
    weight = jnp.where(allowed[None, None], jnp.exp(score - new_top[..., None]), 0.0)
    total = jnp.sum(weight, axis=-1)
    update = jnp.einsum(
        "hgqk,khd->qhgd",
        weight.astype(jnp.bfloat16),
        value_piece.reshape(count, kv_heads, DH),
        preferred_element_type=jnp.float32,
    )
    summed = update
    top, total, summed = (new_top, total, summed)
    result = summed / jnp.transpose(total, (2, 0, 1))[..., None]
    result = result.astype(jnp.bfloat16).reshape(rows, heads * DH)
    own = lax.all_to_all(result, "mp", split_axis=0, concat_axis=1, tiled=True)
    moved = from_behind(own, "section", 1)
    return (own[None], moved[None])


def solution(mesh):
    return jax.shard_map(
        body,
        mesh=mesh,
        in_specs=(
            P("section", "ctx", "mp"),
            P("section", "ctx", "mp"),
            P("section", "ctx", "mp"),
            P("section", None),
        ),
        out_specs=(P("section", ("ctx", "mp"), None), P("section", ("ctx", "mp"), None)),
        check_vma=False,
    )
```

profile of v0, /device:TPU:4, one launch (start us, length us, event | category | flops | bytes accessed | tf_op | source)
XLA Modules:
  0.0 209.2 jit_solution(6878893363365230713)
XLA Ops:
  7.2 0.0 all-gather.5.cloned.1.call-start
  7.2 0.7 all-gather.5.cloned.1.call-update
  7.9 0.0 all-gather.7.cloned.1.call-start
  7.9 0.7 all-gather.7.cloned.1.call-update
  8.7 0.7 copy.19
  9.4 0.1 reduce.2
  9.5 0.2 convert_reduce_fusion
  9.7 0.1 convert_reduce_fusion.1
  9.8 3.7 %fusion.7 = pred[256,8192]{0,1:T(8,128)(4,1)S(1)} fusion(s32[256]{0:T(256)S(1)} %iota_add_fusion, s32[256]{0:T(256)S(1)} %convert_reduce_fusion.1, s32[8192]{0:T(1024)S(1)} %convert_reduce_fusion), kind=kLoop, calls=%fused_computation.10 | loop fusion | flops 6291456 | bytes 2131968 | tf_op jit(solution)/shard_map/and | solution.py:57
  13.5 0.7 select_reduce_fusion
  14.3 1.1 copy.27
  15.4 61.5 %all-gather.5.cloned.1.call-done = bf16[1,8192,128]{2,1,0:T(8,128)(2,1)} async-done(((bf16[1,256,128]{2,1,0:T(8,128)(2,1)}), bf16[1,8192,128]{2,1,0:T(8,128)(2,1)}) %all-gather.5.cloned.1.call-update) | async-done | bytes 2097168 | tf_op jit(solution)/shard_map/all_gather | solution.py:43
  76.9 24.9 %fusion = (f32[8,256]{1,0:T(8,128)S(1)}, f32[8192,256,8]{1,0,2:T(8,128)}) fusion(f32[256]{0:T(256)S(1)} %maximum_multiply_fusion, pred[256,8192]{0,1:T(8,128)(4,1)S(1)} %fusion.7, bf16[256,8,128]{2,1,0:T(8,128)(2,1)S(1)} %bitcast.88, bf16[1,8192,128]{2,1,0:T(8,128)(2,1)} %all-gather.5.cloned.1.call-done), kind=kOutput, calls=%fused_computation.3 | convolution fusion | flops 4345296896 | bytes 71836672 | tf_op jit(solution)/shard_map/qhgd,khd->hgqk/dot_general | solution.py:49
  101.8 21.9 %fusion.1 = f32[8,256]{1,0:T(8,128)S(1)} fusion(f32[8192,256,8]{1,0,2:T(8,128)} %get-tuple-element.3, f32[8,256]{1,0:T(8,128)S(1)} %broadcast_maximum_fusion, f32[256]{0:T(256)S(1)} %maximum_multiply_fusion, pred[256,8192]{0,1:T(8,128)(4,1)S(1)} %fusion.7), kind=kLoop, calls=%fused_computation.4 | loop fusion | flops 83884032 | bytes 69223424 | tf_op jit(solution)/shard_map/reduce_sum | solution.py:64
  123.7 19.1 %all-gather.7.cloned.1.call-done = bf16[1,8192,128]{2,1,0:T(8,128)(2,1)} async-done(((bf16[1,256,128]{2,1,0:T(8,128)(2,1)}), bf16[1,8192,128]{2,1,0:T(8,128)(2,1)}) %all-gather.7.cloned.1.call-update) | async-done | bytes 2097168 | tf_op jit(solution)/shard_map/all_gather | solution.py:44
  142.8 29.6 %divide_convert_fusion = bf16[256,1,8,128]{3,0,2,1:T(8,128)(2,1)S(1)} fusion(bf16[1,8192,128]{2,1,0:T(8,128)(2,1)} %all-gather.7.cloned.1.call-done, f32[8192,256,8]{1,0,2:T(8,128)} %get-tuple-element.3, f32[8,256]{1,0:T(8,128)S(1)} %broadcast_maximum_fusion, f32[256]{0:T(256)S(1)} %maximum_multiply_fusion, pred[256,8192]{0,1:T(8,128)(4,1)S(1)} %fusion.7, ...), kind=kOutput, calls=%fused_computation.15 | convolution fusion | flops 4379377664 | bytes 71844864 | tf_op jit(solution)/shard_map/hgqk,khd->qhgd/dot_general | solution.py:65
  172.4 0.3 copy.22
  172.8 0.2 all_to_all.14
  173.0 14.0 %all_to_all.19 = bf16[4,64,1024]{2,1,0:T(8,128)(2,1)S(1)} all-to-all(bf16[4,64,1024]{2,1,0:T(8,128)(2,1)S(1)} %all_to_all.14), channel_id=1, replica_groups=mesh['section'=2,'ctx'=32,'mp'=4] {'mp'}, dimensions={0} | all-to-all | bytes 1048576 | tf_op jit(solution)/shard_map/all_to_all | solution.py:75
  187.0 0.9 collective-permute-start
  187.9 0.4 copy.23
  188.3 1.2 broadcast_in_dim.64
  189.5 12.0 %collective-permute-done = bf16[64,4096]{1,0:T(8,128)(2,1)S(1)} collective-permute-done((bf16[64,4096]{1,0:T(8,128)(2,1)S(1)}, bf16[64,4096]{1,0:T(8,128)(2,1)S(1)}, u32[]{:S(2)}, u32[]{:S(2)}) %collective-permute-start) | collective-permute-done | bytes 524320 | tf_op jit(solution)/shard_map/ppermute | solution.py:14
  201.5 0.8 copy.33
  (5 shorter events, 0.1 us)
Async XLA Ops:
  7.2 69.7 %all-gather.5.cloned.1.call-start = ((), (), s32[]{:S(2)}) async-start(), calls=%async_computation.1 | async-start | bytes 2162688 | tf_op jit(solution)/shard_map/all_gather | solution.py:43
  7.9 134.9 %all-gather.7.cloned.1.call-start = ((), (), s32[]{:S(2)}) async-start(), calls=%async_computation.2 | async-start | bytes 2162688 | tf_op jit(solution)/shard_map/all_gather | solution.py:44
  187.0 14.5 %collective-permute-start = (bf16[64,4096]{1,0:T(8,128)(2,1)S(1)}, bf16[64,4096]{1,0:T(8,128)(2,1)S(1)}, u32[]{:S(2)}, u32[]{:S(2)}) collective-permute-start(bf16[64,4096]{1,0:T(8,128)(2,1)S(1)} %bitcast.87), channel_id=1, source_target_pairs={{128,0},{0,128},{129,1},{1,129},{130,2},{2,130},{131,3},{3,131},{1... | collective-permute-start | bytes 1572872 | tf_op jit(solution)/shard_map/ppermute | solution.py:14
Sparse Core Ops, SparseCore 0:
  9.8 67.0 all-gather.4
  78.8 63.9 all-gather.6
where the time goes:
time: 209 us
  waiting for transfers between devices  93.9 us (45%)
  matrix products  54.5 us (26%)
  other arithmetic  26.8 us (13%)
  between operations  14.1 us (7%)
  blocking collectives  14 us (7%)
  local copies, waits for them, and re-layouts  4.85 us (2%)
    all_gather x1, waiting for transfers between devices, body(): key_piece = lax.all_gather(key_rows, 'ctx', axis=0, tiled=True)  61.5 us
    dot_general x1, matrix products, body(): jnp.einsum('hgqk,khd->qhgd', weight.astype(jnp.bfloat16), value_piece.res...  29.6 us
    dot_general x1, matrix products, body(): jnp.einsum('qhgd,khd->hgqk', query_heads, key_piece.reshape(count, kv_hea...  24.9 us
    reduce_sum x1, other arithmetic, body(): total = jnp.sum(weight, axis=-1)  21.9 us
    all_gather x1, waiting for transfers between devices, body(): value_piece = lax.all_gather(value_rows, 'ctx', axis=0, tiled=True)  19.1 us
    all_to_all x1, blocking collectives, body(): own = lax.all_to_all(result, 'mp', split_axis=0, concat_axis=1, tiled=True)  14 us
    ppermute x1, waiting for transfers between devices, from_behind(): return lax.ppermute(block, axis, route)  12 us
  transfers between devices with their start and end apart: 3, of which 3 were waited for; matrix products, arithmetic and copies ran while one was open for 26% of the time, Pallas kernels for 0%

commit v1 on v0

--- a/solution.py
+++ b/solution.py
@@ -40,7 +40,9 @@
         1.0 / math.sqrt(DH)
     )
     query_heads = query_rows.reshape(rows, kv_heads, group, DH)
-    key_piece = lax.all_gather(key_rows, "ctx", axis=0, tiled=True)
+    key_piece = jnp.concatenate(
+        lax.all_to_all(jnp.stack([key_rows] * lax.axis_size("ctx")), "ctx", 0, 0), axis=0
+    )
     value_piece = lax.all_gather(value_rows, "ctx", axis=0, tiled=True)
     top = jnp.full((kv_heads, group, rows), -1e30, jnp.float32)
     count = key_piece.shape[0]

time: 209 us -> 191 us (0.914)
  waiting for transfers between devices: 93.9 us -> 62.9 us
  starting transfers between devices: 1 us -> 10.5 us
  local copies, waits for them, and re-layouts: 4.85 us -> 7.51 us
    all_gather x1 -> x0, waiting for transfers between devices: 61.5 us -> none  [body(): key_piece = lax.all_gather(key_rows, 'ctx', axis=0, tiled=True)]
    all_to_all x0 -> x1, waiting for transfers between devices: none -> 50.5 us  [body(): lax.all_to_all(jnp.stack([key_rows] * lax.axis_size('ctx')), 'ctx', 0, 0)]
    all_gather x1, waiting for transfers between devices: 19.1 us -> 0.02 us  [body(): value_piece = lax.all_gather(value_rows, 'ctx', axis=0, tiled=True)]
    all_to_all x0 -> x1, starting transfers between devices: none -> 9.62 us  [body(): lax.all_to_all(jnp.stack([key_rows] * lax.axis_size('ctx')), 'ctx', 0, 0)]
    another operation x1 -> x2, local copies, waits for them, and re-layouts: 0.73 us -> 3.4 us  [the longest x1 2.66 us: body(): jnp.stack([key_rows] * lax.axis_size('ctx'))]
  transfers between devices with their start and end apart: 3 -> 3, of which waited for: 3 -> 2; matrix products, arithmetic and copies ran while one was open for 26% -> 29% of each run, Pallas kernels for 0% -> 0%
where the time goes in v1:
time: 191 us; the launch traced here: 190 us
  waiting for transfers between devices  62.9 us (33%)
  matrix products  54.5 us (29%)
  other arithmetic  26.6 us (14%)
  between operations  14.1 us (7%)
  blocking collectives  14 us (7%)
  starting transfers between devices  10.5 us (5%)
  local copies, waits for them, and re-layouts  7.51 us (4%)
    all_to_all x1, waiting for transfers between devices, body(): lax.all_to_all(jnp.stack([key_rows] * lax.axis_size('ctx')), 'ctx', 0, 0)  50.5 us
    dot_general x1, matrix products, body(): jnp.einsum('hgqk,khd->qhgd', weight.astype(jnp.bfloat16), value_piece.res...  29.7 us
    dot_general x1, matrix products, body(): jnp.einsum('qhgd,khd->hgqk', query_heads, key_piece.reshape(count, kv_hea...  24.8 us
    reduce_sum x1, other arithmetic, body(): total = jnp.sum(weight, axis=-1)  21.7 us
    all_to_all x1, blocking collectives, body(): own = lax.all_to_all(result, 'mp', split_axis=0, concat_axis=1, tiled=True)  14 us
    ppermute x1, waiting for transfers between devices, from_behind(): return lax.ppermute(block, axis, route)  11.6 us
    all_to_all x1, starting transfers between devices, body(): lax.all_to_all(jnp.stack([key_rows] * lax.axis_size('ctx')), 'ctx', 0, 0)  9.62 us
  transfers between devices with their start and end apart: 3, of which 2 were waited for; matrix products, arithmetic and copies ran while one was open for 29% of the time, Pallas kernels for 0%

profile of v1, /device:TPU:4, one launch (start us, length us, event | category | flops | bytes accessed | tf_op | source)
XLA Modules:
  0.0 190.2 jit_solution(7032499518574587754)
XLA Ops:
  7.2 2.7 %stack.3 = bf16[32,256,128]{2,1,0:T(8,128)(2,1)} broadcast(bf16[256,128]{1,0:T(8,128)(2,1)} %bitcast.88), dimensions={1,2} | broadcast | bytes 2162688 | tf_op jit(solution)/shard_map/stack | solution.py:44
  9.8 9.6 %all-to-all-start = ((bf16[32,256,128]{2,1,0:T(8,128)(2,1)}), bf16[32,256,128]{2,1,0:T(8,128)(2,1)}, u32[]{:S(2)}, u32[]{:S(2)}) async-start(bf16[32,256,128]{2,1,0:T(8,128)(2,1)} %stack.3), calls=%async_computation | async-start | bytes 4194304 | tf_op jit(solution)/shard_map/all_to_all | solution.py:44
  19.5 0.0 all-gather.3.cloned.1.call-start
  19.5 0.7 all-gather.3.cloned.1.call-update
  20.2 0.7 copy.19
  21.0 0.1 reduce.2
  21.1 1.1 copy.27
  22.2 0.1 convert_reduce_fusion.1
  22.3 0.7 select_reduce_fusion
  23.1 0.2 convert_reduce_fusion
  23.3 3.7 %fusion.7 = pred[256,8192]{0,1:T(8,128)(4,1)S(1)} fusion(s32[256]{0:T(256)S(1)} %iota_add_fusion, s32[256]{0:T(256)S(1)} %convert_reduce_fusion.1, s32[8192]{0:T(1024)S(1)} %convert_reduce_fusion), kind=kLoop, calls=%fused_computation.10 | loop fusion | flops 6291456 | bytes 2131968 | tf_op jit(solution)/shard_map/and | solution.py:59
  27.0 50.5 %all-to-all-done = bf16[32,256,128]{2,1,0:T(8,128)(2,1)} async-done(((bf16[32,256,128]{2,1,0:T(8,128)(2,1)}), bf16[32,256,128]{2,1,0:T(8,128)(2,1)}, u32[]{:S(2)}, u32[]{:S(2)}) %all-to-all-start) | async-done | bytes 2097184 | tf_op jit(solution)/shard_map/all_to_all | solution.py:44
  77.5 24.8 %fusion = (f32[8,256]{1,0:T(8,128)S(1)}, f32[8192,256,8]{1,0,2:T(8,128)}) fusion(f32[256]{0:T(256)S(1)} %maximum_multiply_fusion, pred[256,8192]{0,1:T(8,128)(4,1)S(1)} %fusion.7, bf16[8192,128,1]{1,0,2:T(8,128)(2,1)} %bitcast.3, bf16[256,8,128]{2,1,0:T(8,128)(2,1)S(1)} %bitcast.85), kind=kOutput, calls=%fused_computation.3 | convolution fusion | flops 4345296896 | bytes 71836672 | tf_op jit(solution)/shard_map/qhgd,khd->hgqk/dot_general | solution.py:51
  102.4 21.7 %fusion.1 = f32[8,256]{1,0:T(8,128)S(1)} fusion(f32[8192,256,8]{1,0,2:T(8,128)} %get-tuple-element.3, f32[8,256]{1,0:T(8,128)S(1)} %broadcast_maximum_fusion, f32[256]{0:T(256)S(1)} %maximum_multiply_fusion, pred[256,8192]{0,1:T(8,128)(4,1)S(1)} %fusion.7), kind=kLoop, calls=%fused_computation.4 | loop fusion | flops 83884032 | bytes 69223424 | tf_op jit(solution)/shard_map/reduce_sum | solution.py:66
  124.1 0.0 all-gather.3.cloned.1.call-done
  124.1 29.7 %divide_convert_fusion = bf16[256,1,8,128]{3,0,2,1:T(8,128)(2,1)S(1)} fusion(bf16[1,8192,128]{2,1,0:T(8,128)(2,1)} %all-gather.3.cloned.1.call-done, f32[8192,256,8]{1,0,2:T(8,128)} %get-tuple-element.3, f32[8,256]{1,0:T(8,128)S(1)} %broadcast_maximum_fusion, f32[256]{0:T(256)S(1)} %maximum_multiply_fusion, pred[256,8192]{0,1:T(8,128)(4,1)S(1)} %fusion.7, ...), kind=kOutput, calls=%fused_computation.13 | convolution fusion | flops 4379377664 | bytes 71844864 | tf_op jit(solution)/shard_map/hgqk,khd->qhgd/dot_general | solution.py:67
  153.8 0.3 copy.22
  154.2 0.2 all_to_all.18
  154.4 14.0 %all_to_all.24 = bf16[4,64,1024]{2,1,0:T(8,128)(2,1)S(1)} all-to-all(bf16[4,64,1024]{2,1,0:T(8,128)(2,1)S(1)} %all_to_all.18), channel_id=1, replica_groups=mesh['section'=2,'ctx'=32,'mp'=4] {'mp'}, dimensions={0} | all-to-all | bytes 1048576 | tf_op jit(solution)/shard_map/all_to_all | solution.py:77
  168.5 0.8 collective-permute-start
  169.3 0.4 copy.23
  169.7 1.2 broadcast_in_dim.64
  170.9 11.6 %collective-permute-done = bf16[64,4096]{1,0:T(8,128)(2,1)S(1)} collective-permute-done((bf16[64,4096]{1,0:T(8,128)(2,1)S(1)}, bf16[64,4096]{1,0:T(8,128)(2,1)S(1)}, u32[]{:S(2)}, u32[]{:S(2)}) %collective-permute-start) | collective-permute-done | bytes 524320 | tf_op jit(solution)/shard_map/ppermute | solution.py:14
  182.5 0.8 copy.33
  (5 shorter events, 0.1 us)
Async XLA Ops:
  9.8 67.7 %all-to-all-start = ((bf16[32,256,128]{2,1,0:T(8,128)(2,1)}), bf16[32,256,128]{2,1,0:T(8,128)(2,1)}, u32[]{:S(2)}, u32[]{:S(2)}) async-start(bf16[32,256,128]{2,1,0:T(8,128)(2,1)} %stack.3), calls=%async_computation | async-start | bytes 4194304 | tf_op jit(solution)/shard_map/all_to_all | solution.py:44
  19.5 104.6 %all-gather.3.cloned.1.call-start = ((), (), s32[]{:S(2)}) async-start(), calls=%async_computation.2 | async-start | bytes 2162688 | tf_op jit(solution)/shard_map/all_gather | solution.py:46
  168.5 14.1 %collective-permute-start = (bf16[64,4096]{1,0:T(8,128)(2,1)S(1)}, bf16[64,4096]{1,0:T(8,128)(2,1)S(1)}, u32[]{:S(2)}, u32[]{:S(2)}) collective-permute-start(bf16[64,4096]{1,0:T(8,128)(2,1)S(1)} %bitcast.87), channel_id=1, source_target_pairs={{128,0},{0,128},{129,1},{1,129},{130,2},{2,130},{131,3},{3,131},{1... | collective-permute-start | bytes 1572872 | tf_op jit(solution)/shard_map/ppermute | solution.py:14
Sparse Core Ops, SparseCore 0:
  22.1 74.4 all-gather.2
